TPU v7x, 256 devices: a whole 4x4x8 slice. The times are simulated.
256 devices in a mesh: wide: 32 (over x, z), narrow: 8 (over y, core).
Axes of the slice: x: 4, y: 4, z: 8, core: 2. Of those that a mesh axis runs over, the one named last changes fastest.
Arguments:
- tensor: bfloat16 [256, 3, 1024, 1024], P('wide', None, 'narrow'), may hold values from -6 to 6
- occupied: bfloat16 [256, 3, 1024], replicated, may hold values from -0.625 to 0.625
- virtual: bfloat16 [256, 3, 1024], replicated, may hold values from -0.0007324219 to 0.0007324219
- atom_size: int32 [256], replicated, may hold values from 14 to 32, as said below
- tensor_pattern: int32 [256, 3], replicated, may hold values 0 or 1
- occupied_pattern: int32 [256, 3], replicated, may hold values 0 or 1
- virtual_pattern: int32 [256, 3], replicated, may hold values 0 or 1
Outputs:
- response: float32 [1024, 1024], P('wide', 'narrow')
Inputs may be any that keep to these rules, and one draw needn't show every extreme that they name: Orbitals of an atom at and beyond its atom_size are padding.
All inputs are finite; a program needn't handle non-finite values.
Results may differ from a plain program's by a relative error of at most 0.0041.
Values may be sent and summed in bfloat16 or wider, within the bound.
No kernel may reach another device: no remote copies, remote signals or barrier semaphores. Data moves between devices by JAX's collectives and lax.ppermute only.
A program may use at most 192 MiB of HBM per device.

v0:
```python
import jax
import jax.numpy as jnp
from jax import lax
from jax.sharding import PartitionSpec as P

BO = 32
CHUNK = 256


def block_masks(size_pad, tensor_flags, occupied_flags, virtual_flags, atom_index):
    nearby_sizes = lax.dynamic_slice(size_pad, (atom_index,), (5,))
    present = (nearby_sizes > 0).astype(jnp.int32)
    orbital = jnp.arange(BO, dtype=jnp.int32)
    zero_index = jnp.zeros((), jnp.int32)
    row_flags = lax.dynamic_slice(tensor_flags, (atom_index + 1, zero_index), (3, 3))
    row_ok = (orbital[None, :] < nearby_sizes[1:4, None]).astype(jnp.int32)
    partner = jnp.stack([nearby_sizes[r : r + 3] for r in range(3)])
    column_ok = (orbital[None, None, :] < partner[:, :, None]).astype(jnp.int32)
    entry_mask = row_flags[:, :, None, None] * row_ok[:, None, :, None] * column_ok[:, :, None, :]
    tensor_mask = entry_mask.reshape(3, 3, 1, BO * BO).astype(jnp.bfloat16)
    occupied_mask = (
        lax.dynamic_slice(occupied_flags, (atom_index + 2, zero_index), (1, 3))[0] * present[1:4]
    )
    partner_present = jnp.stack([present[r : r + 3] for r in range(3)])
    virtual_mask = (
        lax.dynamic_slice(virtual_flags, (atom_index + 1, zero_index), (3, 3))
        * present[1:4, None]
        * partner_present
    )
    return (tensor_mask, occupied_mask.astype(jnp.bfloat16), virtual_mask.astype(jnp.bfloat16))


def left_kron(block, row_mask):
    size = BO * BO
    spread = jnp.repeat(block.T, BO, axis=1)
    full = jnp.broadcast_to(spread[:, None, :], (BO, BO, size)).reshape(size, size)
    rows = lax.broadcasted_iota(jnp.int32, (size, size), 0)
    columns = lax.broadcasted_iota(jnp.int32, (size, size), 1)
    keep = (rows % BO) == (columns % BO)
    return (jnp.where(keep, full, 0.0) * row_mask[:, None]).astype(jnp.bfloat16)


def right_kron(block, row_mask):
    size = BO * BO
    spread = jnp.tile(block, (1, BO))
    full = jnp.broadcast_to(spread[None, :, :], (BO, BO, size)).reshape(size, size)
    rows = lax.broadcasted_iota(jnp.int32, (size, size), 0)
    columns = lax.broadcasted_iota(jnp.int32, (size, size), 1)
    keep = (rows // BO) == (columns // BO)
    return (jnp.where(keep, full, 0.0) * row_mask[:, None]).astype(jnp.bfloat16)


def right_kron_chunks(block, row_mask, chunk):
    groups = chunk // BO
    spread = jnp.tile(block, (1, groups))
    full = jnp.broadcast_to(spread[None, :, :], (groups, BO, chunk)).reshape(chunk, chunk)
    rows = lax.broadcasted_iota(jnp.int32, (chunk, chunk), 0)
    columns = lax.broadcasted_iota(jnp.int32, (chunk, chunk), 1)
    keep = (rows // BO) == (columns // BO)
    sized = jnp.where(keep, full, 0.0)
    masks = row_mask.reshape(-1, chunk)
    return (sized[None] * masks[:, :, None]).astype(jnp.bfloat16)


def contract(rows, tensor_mask, occupied_row, virtual_rows):
    occupied_blocks = occupied_row.reshape(3, BO, BO).astype(jnp.float32)
    virtual_blocks = virtual_rows.reshape(3, 3, BO, BO).astype(jnp.float32)
    row_masks = tensor_mask.reshape(3, 3, BO * BO).astype(jnp.float32)
    occupied_terms = []
    virtual_terms = []
    for out_band in range(5):
        total_left = None
        total_right = None
        for left_band in range(3):
            right_band = out_band - left_band
            if 0 <= right_band < 3:
                left = jnp.dot(
                    rows[left_band][right_band],
                    left_kron(occupied_blocks[left_band], row_masks[left_band, right_band]),
                    preferred_element_type=jnp.float32,
                )
                source = rows[1][left_band]
                pieces = right_kron_chunks(virtual_blocks[left_band, right_band], row_masks[1, left_band], CHUNK)
                right = jnp.concatenate(
                    [
                        jnp.dot(
                            source[:, piece * CHUNK : (piece + 1) * CHUNK],
                            pieces[piece],
                            preferred_element_type=jnp.float32,
                        )
                        for piece in range(pieces.shape[0])
                    ],
                    1,
                )
                total_left = left if total_left is None else total_left + left
                total_right = right if total_right is None else total_right + right
        occupied_terms.append(total_left.astype(jnp.bfloat16))
        virtual_terms.append(total_right.astype(jnp.bfloat16))
    left_product = jnp.concatenate(occupied_terms, 1)
    right_product = jnp.concatenate(virtual_terms, 1)
    return (left_product, right_product)


def neighbours(array, axis):
    devices = lax.axis_size(axis)
    up = [(i, (i + 1) % devices) for i in range(devices - 1)]
    down = [(j, i) for i, j in up]
    before = lax.ppermute(array, axis, up)
    after = lax.ppermute(array, axis, down)
    return before, after


def body(tensor, occupied, virtual, atom_size, tensor_pattern, occupied_pattern, virtual_pattern):
    narrow_count = lax.axis_size("narrow")
    atom_index = lax.axis_index("wide") * narrow_count + lax.axis_index("narrow")
    sectioned_rows = tensor[:, None]
    regrouped = lax.all_to_all(sectioned_rows, "narrow", split_axis=0, concat_axis=3, tiled=True)
    own = regrouped[0, 0]
    before, after = neighbours(own, ("wide", "narrow"))
    occupied_pad = jnp.pad(occupied, ((1, 1), (0, 0), (0, 0)))
    virtual_pad = jnp.pad(virtual, ((1, 1), (0, 0), (0, 0)))
    size_pad = jnp.pad(atom_size, 2)
    tensor_flags = jnp.pad(tensor_pattern, ((2, 2), (0, 0)))
    occupied_flags = jnp.pad(occupied_pattern, ((2, 2), (0, 0)))
    virtual_flags = jnp.pad(virtual_pattern, ((2, 2), (0, 0)))
    tensor_mask, occupied_mask, virtual_mask = block_masks(
        size_pad, tensor_flags, occupied_flags, virtual_flags, atom_index
    )
    occupied_row = (
        lax.dynamic_slice_in_dim(occupied_pad, atom_index + 1, 1, 0)[0] * occupied_mask[:, None]
    )
    virtual_rows = (
        lax.dynamic_slice_in_dim(virtual_pad, atom_index, 3, 0) * virtual_mask[:, :, None]
    )
    left_product, right_product = contract(
        (before, own, after), tensor_mask, occupied_row, virtual_rows
    )
    partial_response = lax.dot_general(
        left_product, right_product, (((1,), (1,)), ((), ())), preferred_element_type=jnp.float32
    )
    column_share = lax.psum_scatter(partial_response, "narrow", scatter_dimension=1, tiled=True)
    wide_count = lax.axis_size("wide")
    row_pieces = column_share.reshape(wide_count, column_share.shape[0] // wide_count, column_share.shape[1])
    gathered = lax.all_to_all(row_pieces, "wide", 0, 0, tiled=True)
    return gathered.sum(0)


def solution(mesh):
    placed = (P("wide", None, "narrow", None), P(), P(), P(), P(), P(), P())
    return jax.shard_map(
        body, mesh=mesh, in_specs=placed, out_specs=P("wide", "narrow"), check_vma=False
    )
```

profile of v0, /device:TPU:57, one launch (start us, length us, event | category | flops | bytes accessed | tf_op | source)
XLA Modules:
  0.0 281.5 jit_solution(15997748231498211613)
XLA Ops:
  6.5 5.3 %all-to-all-start = ((bf16[8,1,3,128,1024]{4,3,2,1,0:T(8,128)(2,1)}), bf16[8,1,3,128,1024]{4,3,2,1,0:T(8,128)(2,1)}, u32[]{:S(2)}, u32[]{:S(2)}) async-start(bf16[8,1,3,128,1024]{4,3,2,1,0:T(8,128)(2,1)} %bitcast.384), calls=%async_computation | async-start | bytes 12582912 | tf_op jit(solution)/shard_map/all_to_all | solution.py:117
  27.1 9.1 %fusion.8 = (bf16[32,32,1024]{2,1,0:T(8,128)(2,1)}, bf16[32,32,1024]{2,1,0:T(8,128)(2,1)}, bf16[32,32,1024]{2,1,0:T(8,128)(2,1)}, bf16[32,32,1024]{2,1,0:T(8,128...) fusion(f32[32,32]{1,0:T(8,128)S(1)} %mul.367, ...), kind=kLoop, calls=%fused_computation.17 | loop fusion | flops 25165824 | bytes 19322880 | tf_op jit(solution)/shard_map/convert_element_type | solution.py:40
  36.2 45.2 %all-to-all-done = bf16[8,1,3,128,1024]{4,3,2,1,0:T(8,128)(2,1)} async-done(((bf16[8,1,3,128,1024]{4,3,2,1,0:T(8,128)(2,1)}), bf16[8,1,3,128,1024]{4,3,2,1,0:T(8,128)(2,1)}, u32[]{:S(2)}, u32[]{:S(2)}) %all-to-all-start) | async-done | bytes 6291488 | tf_op jit(solution)/shard_map/all_to_all | solution.py:117
  81.4 3.5 %copy.27 = bf16[8,1,3,128,1024]{4,3,0,2,1:T(8,128)(2,1)S(1)} copy(bf16[8,1,3,128,1024]{4,3,2,1,0:T(8,128)(2,1)} %all-to-all-done) | data formatting | bytes 12582912 | tf_op jit(solution)/shard_map/all_to_all | solution.py:117
  84.9 5.9 %collective-permute-start = (bf16[3,1024,1024]{2,1,0:T(8,128)(2,1)S(1)}, bf16[3,1024,1024]{2,1,0:T(8,128)(2,1)}, u32[]{:S(2)}, u32[]{:S(2)}) collective-permute-start(bf16[3,1024,1024]{2,1,0:T(8,128)(2,1)S(1)} %bitcast.355), channel_id=1, source_target_pairs={{0,1},{1,2},{2,3},{3,4},{4,5},{5,6},{6,7},{7,8},{8,9},{9,10},{10,1... | collective-permute-start | bytes 18874376 | tf_op jit(solution)/shard_map/ppermute | solution.py:108
  90.8 2.1 collective-permute-start.1
  100.2 2.4 convolution_bitcast_fusion.15
  119.4 1.4 convolution_bitcast_fusion.6
  123.3 1.8 fusion.21
  125.1 4.2 %fusion.20 = bf16[1024,5120]{0,1:T(8,128)(2,1)} fusion(bf16[1024,5120]{0,1:T(8,128)(2,1)} %fusion.21, f32[1024,256]{0,1:T(8,128)S(1)} %convolution_bitcast_fusion.8, f32[1024,256]{0,1:T(8,128)S(1)} %convolution_bitcast_fusion.9, f32[1024,256]{0,1:T(8,128)S(1)} %convolution_bitcast_fusion.10, f32[1024,256]{0,1:T(8,128)S(1)} %convolution_bitcast_fusion.11, ...), kind=kLoop, calls=%fused_computation.36 | loop fusion | flops 12582912 | bytes 14680064
  129.2 5.0 %fusion.19 = bf16[1024,5120]{0,1:T(8,128)(2,1)} fusion(bf16[1024,5120]{0,1:T(8,128)(2,1)} %fusion.20, f32[1024,256]{0,1:T(8,128)} %convolution_bitcast_fusion, f32[1024,256]{0,1:T(8,128)} %convolution_bitcast_fusion.1, f32[1024,256]{0,1:T(8,128)} %convolution_bitcast_fusion.2, f32[1024,256]{0,1:T(8,128)} %convolution_bitcast_fusion.3, ...), kind=kLoop, calls=%fused_computation.35 | loop fusion | flops 8388608 | bytes 10485760
  139.0 4.4 %fusion.95 = f32[1024,1024]{1,0:T(8,128)} fusion(bf16[1024,1024]{1,0:T(8,128)(2,1)S(1)} %bitcast.393, bf16[1024,1024]{1,0:T(8,128)(2,1)S(1)} %bitcast.383), kind=kOutput, calls=%fused_computation.262 | convolution fusion | flops 2147483648 | bytes 8388608 | tf_op jit(solution)/shard_map/dot_general | solution.py:77
  143.4 2.4 fusion.96
  145.8 2.4 fusion.97
  148.2 10.5 %collective-permute-done = bf16[3,1024,1024]{2,1,0:T(8,128)(2,1)} collective-permute-done((bf16[3,1024,1024]{2,1,0:T(8,128)(2,1)S(1)}, bf16[3,1024,1024]{2,1,0:T(8,128)(2,1)}, u32[]{:S(2)}, u32[]{:S(2)}) %collective-permute-start) | collective-permute-done | bytes 6291488 | tf_op jit(solution)/shard_map/ppermute | solution.py:108
  158.7 4.1 %bitcast_dynamic-update-slice_fusion.1 = bf16[1024,5120]{0,1:T(8,128)(2,1)S(1)} fusion(bf16[1024,1024]{1,0:T(8,128)(2,1)S(1)} %bitcast.390, bf16[3,1024,1024]{2,1,0:T(8,128)(2,1)} %collective-permute-done), kind=kOutput, calls=%fused_computation.51 | convolution fusion | flops 2148532224 | bytes 6291456 | tf_op jit(solution)/shard_map/dot_general | solution.py:77
  162.9 6.6 %fusion.25 = f32[1024,1024]{1,0:T(8,128)} fusion(bf16[1024,1024]{1,0:T(8,128)(2,1)S(1)} %bitcast.389, bf16[3,1024,1024]{2,1,0:T(8,128)(2,1)} %collective-permute-done), kind=kOutput, calls=%fused_computation.45 | convolution fusion | flops 2147483648 | bytes 8388608 | tf_op jit(solution)/shard_map/dot_general | solution.py:77
  169.5 5.4 %fusion.14 = bf16[1024,5120]{0,1:T(8,128)(2,1)S(1)} fusion(bf16[1024,5120]{0,1:T(8,128)(2,1)S(1)} %bitcast_dynamic-update-slice_fusion.1, f32[1024,1024]{1,0:T(8,128)} %fusion.95, bf16[1024,1024]{1,0:T(8,128)(2,1)S(1)} %bitcast.388, bf16[3,1024,1024]{2,1,0:T(8,128)(2,1)} %collective-permute-done), kind=kOutput, calls=%fused_computation.30 | convolution fusion | flops 2149580800 | bytes 10485760 | tf_op jit(solution)/shard_map/dot_general | solution.py:77
  174.9 5.5 %fusion.16 = bf16[1024,5120]{0,1:T(8,128)(2,1)S(1)} fusion(bf16[1024,5120]{0,1:T(8,128)(2,1)S(1)} %fusion.14, f32[1024,1024]{1,0:T(8,128)} %fusion.25, f32[1024,1024]{1,0:T(8,128)S(1)} %fusion.96, bf16[1024,1024]{1,0:T(8,128)(2,1)S(1)} %bitcast.387, bf16[3,1024,1024]{2,1,0:T(8,128)(2,1)} %collective-permute-done.1), kind=kOutput, calls=%fused_computation.32 | convolution fusion | flops 2150629376 | bytes 14680064 | tf_op jit(solution)/shard_map/dot_general | solution.py:77
  180.4 4.2 %fusion.18 = bf16[1024,5120]{0,1:T(8,128)(2,1)S(1)} fusion(bf16[1024,5120]{0,1:T(8,128)(2,1)S(1)} %fusion.16, f32[1024,1024]{1,0:T(8,128)S(1)} %fusion.97, bf16[1024,1024]{1,0:T(8,128)(2,1)S(1)} %bitcast.386, bf16[3,1024,1024]{2,1,0:T(8,128)(2,1)} %collective-permute-done.1), kind=kOutput, calls=%fused_computation.34 | convolution fusion | flops 2149580800 | bytes 10485760 | tf_op jit(solution)/shard_map/dot_general | solution.py:77
  184.6 4.0 %bitcast_dynamic-update-slice_fusion = bf16[1024,5120]{0,1:T(8,128)(2,1)S(1)} fusion(bf16[1024,5120]{0,1:T(8,128)(2,1)S(1)} %fusion.18, bf16[1024,1024]{1,0:T(8,128)(2,1)S(1)} %bitcast.385, bf16[3,1024,1024]{2,1,0:T(8,128)(2,1)} %collective-permute-done.1), kind=kOutput, calls=%fused_computation.50 | convolution fusion | flops 2148532224 | bytes 6291456 | tf_op jit(solution)/shard_map/dot_general | solution.py:77
  188.6 15.2 %fusion.98 = f32[1024,1024]{1,0:T(8,128)} fusion(bf16[1024,5120]{0,1:T(8,128)(2,1)S(1)} %bitcast_dynamic-update-slice_fusion, bf16[1024,5120]{0,1:T(8,128)(2,1)} %fusion.43), kind=kOutput, calls=%fused_computation.265 | convolution fusion | flops 10737418240 | bytes 25165824 | tf_op jit(solution)/shard_map/dot_general | solution.py:138
  203.9 42.8 %reduce-scatter.2.cloned.1.call-done = f32[1024,128]{1,0:T(8,128)} async-done(((f32[1024,1024]{1,0:T(8,128)}), f32[1024,128]{1,0:T(8,128)}) %reduce-scatter.2.cloned.1.call-update) | async-done | bytes 524304 | tf_op jit(solution)/shard_map/reduce_scatter | solution.py:141
  246.6 27.1 %all_to_all.20 = f32[32,32,128]{2,1,0:T(8,128)S(1)} all-to-all(f32[32,32,128]{2,1,0:T(8,128)} %bitcast.394), channel_id=1, replica_groups=mesh['wide'=32,'narrow'=8] {'wide'}, dimensions={0} | all-to-all | bytes 1048576 | tf_op jit(solution)/shard_map/all_to_all | solution.py:144
  (172 shorter events, 46.8 us)
Async XLA Ops:
  6.5 5.4 %copy-start.29 = (s32[256,3]{0,1:T(4,128)S(1)}, s32[256,3]{0,1:T(4,128)}, u32[]{:S(2)}) copy-start(s32[256,3]{0,1:T(4,128)} %param.11) | copy-start | bytes 9220
  6.5 5.6 %copy-start.28 = (s32[256,3]{0,1:T(4,128)S(1)}, s32[256,3]{0,1:T(4,128)}, u32[]{:S(2)}) copy-start(s32[256,3]{0,1:T(4,128)} %param.12) | copy-start | bytes 9220
  6.5 5.8 %copy-start.30 = (s32[256]{0:T(256)S(1)}, s32[256]{0:T(256)}, u32[]{:S(2)}) copy-start(s32[256]{0:T(256)} %param.10) | copy-start | bytes 3076
  6.5 6.6 %copy-start.12 = (bf16[256,3,1024]{2,0,1:T(8,128)(2,1)S(1)}, bf16[256,3,1024]{2,0,1:T(8,128)(2,1)}, u32[]{:S(2)}) copy-start(bf16[256,3,1024]{2,0,1:T(8,128)(2,1)} %param.8) | copy-start | bytes 4718596
  6.5 74.9 %all-to-all-start = ((bf16[8,1,3,128,1024]{4,3,2,1,0:T(8,128)(2,1)}), bf16[8,1,3,128,1024]{4,3,2,1,0:T(8,128)(2,1)}, u32[]{:S(2)}, u32[]{:S(2)}) async-start(bf16[8,1,3,128,1024]{4,3,2,1,0:T(8,128)(2,1)} %bitcast.384), calls=%async_computation | async-start | bytes 12582912 | tf_op jit(solution)/shard_map/all_to_all | solution.py:117
  11.9 10.3 %copy-start.27 = (s32[256,3]{0,1:T(4,128)S(1)}, s32[256,3]{0,1:T(4,128)}, u32[]{:S(2)}) copy-start(s32[256,3]{0,1:T(4,128)} %param.13) | copy-start | bytes 9220
  11.9 10.7 %copy-start.13 = (bf16[256,3,1024]{2,0,1:T(8,128)(2,1)S(1)}, bf16[256,3,1024]{2,0,1:T(8,128)(2,1)}, u32[]{:S(2)}) copy-start(bf16[256,3,1024]{2,0,1:T(8,128)(2,1)} %param.9) | copy-start | bytes 4718596
  11.9 234.8 %reduce-scatter.2.cloned.1.call-start = ((), (), s32[]{:S(2)}) async-start(), calls=%async_computation.3 | async-start | bytes 4718592 | tf_op jit(solution)/shard_map/reduce_scatter | solution.py:141
  24.1 2.9 %copy-start.14 = (f32[32,1024]{1,0:T(8,128)S(1)}, f32[32,1024]{1,0:T(8,128)}, u32[]{:S(2)}) copy-start(f32[32,1024]{1,0:T(8,128)} %broadcast_in_dim.71) | copy-start | bytes 393220
  25.7 72.9 %copy-start.11 = (bf16[4,256,256]{2,1,0:T(8,128)(2,1)}, bf16[4,256,256]{2,1,0:T(8,128)(2,1)S(1)}, u32[]{:S(2)}) copy-start(bf16[4,256,256]{2,1,0:T(8,128)(2,1)S(1)} %get-tuple-element.64) | copy-start | bytes 1572868
  84.9 73.8 %collective-permute-start = (bf16[3,1024,1024]{2,1,0:T(8,128)(2,1)S(1)}, bf16[3,1024,1024]{2,1,0:T(8,128)(2,1)}, u32[]{:S(2)}, u32[]{:S(2)}) collective-permute-start(bf16[3,1024,1024]{2,1,0:T(8,128)(2,1)S(1)} %bitcast.355), channel_id=1, source_target_pairs={{0,1},{1,2},{2,3},{3,4},{4,5},{5,6},{6,7},{7,8},{8,9},{9,10},{10,1... | collective-permute-start | bytes 18874376 | tf_op jit(solution)/shard_map/ppermute | solution.py:108
  90.8 84.1 %collective-permute-start.1 = (bf16[3,1024,1024]{2,1,0:T(8,128)(2,1)S(1)}, bf16[3,1024,1024]{2,1,0:T(8,128)(2,1)}, u32[]{:S(2)}, u32[]{:S(2)}) collective-permute-start(bf16[3,1024,1024]{2,1,0:T(8,128)(2,1)S(1)} %bitcast.356), channel_id=1, source_target_pairs={{1,0},{2,1},{3,2},{4,3},{5,4},{6,5},{7,6},{8,7},{9,8},{10,9},{11,1... | collective-permute-start | bytes 18874376 | tf_op jit(solution)/shard_map/ppermute | solution.py:109
  97.9 4.7 %copy-start.9 = (bf16[4,256,256]{2,1,0:T(8,128)(2,1)S(1)}, bf16[4,256,256]{2,1,0:T(8,128)(2,1)}, u32[]{:S(2)}) copy-start(bf16[4,256,256]{2,1,0:T(8,128)(2,1)} %get-tuple-element.66) | copy-start | bytes 1572868
  100.2 7.7 %copy-start.18 = (bf16[4,256,256]{2,1,0:T(8,128)(2,1)S(1)}, bf16[4,256,256]{2,1,0:T(8,128)(2,1)}, u32[]{:S(2)}) copy-start(bf16[4,256,256]{2,1,0:T(8,128)(2,1)} %get-tuple-element.68) | copy-start | bytes 1572868
  103.9 7.4 %copy-start.10 = (bf16[4,256,256]{2,1,0:T(8,128)(2,1)S(1)}, bf16[4,256,256]{2,1,0:T(8,128)(2,1)}, u32[]{:S(2)}) copy-start(bf16[4,256,256]{2,1,0:T(8,128)(2,1)} %get-tuple-element.61) | copy-start | bytes 1572868
  129.2 5.0 %copy-start.17 = (bf16[4,256,256]{2,1,0:T(8,128)(2,1)S(1)}, bf16[4,256,256]{2,1,0:T(8,128)(2,1)}, u32[]{:S(2)}) copy-start(bf16[4,256,256]{2,1,0:T(8,128)(2,1)} %get-tuple-element.60) | copy-start | bytes 1572868
  134.3 4.7 %copy-start.8 = (bf16[32,32,1024]{2,1,0:T(8,128)(2,1)S(1)}, bf16[32,32,1024]{2,1,0:T(8,128)(2,1)}, u32[]{:S(2)}) copy-start(bf16[32,32,1024]{2,1,0:T(8,128)(2,1)} %get-tuple-element.54) | copy-start | bytes 6291460
  139.0 4.4 %copy-start.7 = (bf16[32,32,1024]{2,1,0:T(8,128)(2,1)S(1)}, bf16[32,32,1024]{2,1,0:T(8,128)(2,1)}, u32[]{:S(2)}) copy-start(bf16[32,32,1024]{2,1,0:T(8,128)(2,1)} %get-tuple-element.55) | copy-start | bytes 6291460
  145.8 12.9 %copy-start.5 = (bf16[32,32,1024]{2,1,0:T(8,128)(2,1)S(1)}, bf16[32,32,1024]{2,1,0:T(8,128)(2,1)}, u32[]{:S(2)}) copy-start(bf16[32,32,1024]{2,1,0:T(8,128)(2,1)} %get-tuple-element.57) | copy-start | bytes 6291460
  158.7 4.1 %copy-start.4 = (bf16[32,32,1024]{2,1,0:T(8,128)(2,1)S(1)}, bf16[32,32,1024]{2,1,0:T(8,128)(2,1)}, u32[]{:S(2)}) copy-start(bf16[32,32,1024]{2,1,0:T(8,128)(2,1)} %get-tuple-element.59) | copy-start | bytes 6291460
  162.9 6.6 %copy-start.3 = (bf16[32,32,1024]{2,1,0:T(8,128)(2,1)S(1)}, bf16[32,32,1024]{2,1,0:T(8,128)(2,1)}, u32[]{:S(2)}) copy-start(bf16[32,32,1024]{2,1,0:T(8,128)(2,1)} %get-tuple-element.58) | copy-start | bytes 6291460
  169.5 5.4 %copy-start.2 = (bf16[32,32,1024]{2,1,0:T(8,128)(2,1)S(1)}, bf16[32,32,1024]{2,1,0:T(8,128)(2,1)}, u32[]{:S(2)}) copy-start(bf16[32,32,1024]{2,1,0:T(8,128)(2,1)} %get-tuple-element.23) | copy-start | bytes 6291460
  174.9 5.5 %copy-start.1 = (bf16[32,32,1024]{2,1,0:T(8,128)(2,1)S(1)}, bf16[32,32,1024]{2,1,0:T(8,128)(2,1)}, u32[]{:S(2)}) copy-start(bf16[32,32,1024]{2,1,0:T(8,128)(2,1)} %get-tuple-element.22) | copy-start | bytes 6291460
  180.4 4.2 %copy-start = (bf16[32,32,1024]{2,1,0:T(8,128)(2,1)S(1)}, bf16[32,32,1024]{2,1,0:T(8,128)(2,1)}, u32[]{:S(2)}) copy-start(bf16[32,32,1024]{2,1,0:T(8,128)(2,1)} %get-tuple-element.21) | copy-start | bytes 6291460
  (11 other events, 31.4 us)
Sparse Core Ops, SparseCore 0:
  204.0 42.6 reduce-scatter.1
where the time goes:
time: 287 us; the launch traced here: 281 us
  waiting for transfers between devices  98.5 us (34%)
  matrix products  88.1 us (31%)
  blocking collectives  27.1 us (9%)
  other arithmetic  24.4 us (9%)
  local copies, waits for them, and re-layouts  15.7 us (5%)
  between operations  14.3 us (5%)
  starting transfers between devices  13.4 us (5%)
    all_to_all x1, waiting for transfers between devices, body(): lax.all_to_all(sectioned_rows, 'narrow', split_axis=0, concat_axis=3, til...  45.2 us
    reduce_scatter x1, waiting for transfers between devices, body(): lax.psum_scatter(partial_response, 'narrow', scatter_dimension=1, tiled=T...  42.8 us
    dot_general x9, matrix products, contract(): jnp.dot(rows[left_band][right_band], left_kron(occupied_blocks[left_band]...  39 us
    dot_general x36, matrix products, contract(): jnp.dot(source[:, piece * CHUNK:(piece + 1) * CHUNK], pieces[piece], pref...  33.9 us
    all_to_all x1, blocking collectives, body(): gathered = lax.all_to_all(row_pieces, 'wide', 0, 0, tiled=True)  27.1 us
    dot_general x1, matrix products, body(): lax.dot_general(left_product, right_product, (((1,), (1,)), ((), ())), pr...  15.2 us
    unnamed x3, other arithmetic  10.9 us
    ppermute x1, waiting for transfers between devices, neighbours(): before = lax.ppermute(array, axis, up)  10.5 us
  transfers between devices with their start and end apart: 4, of which 3 were waited for; matrix products, arithmetic and copies ran while one was open for 34% of the time, Pallas kernels for 0%

commit v1 on v0

--- a/solution.py
+++ b/solution.py
@@ -138,10 +138,13 @@
     partial_response = lax.dot_general(
         left_product, right_product, (((1,), (1,)), ((), ())), preferred_element_type=jnp.float32
     )
-    column_share = lax.psum_scatter(partial_response, "narrow", scatter_dimension=1, tiled=True)
     wide_count = lax.axis_size("wide")
-    row_pieces = column_share.reshape(wide_count, column_share.shape[0] // wide_count, column_share.shape[1])
-    gathered = lax.all_to_all(row_pieces, "wide", 0, 0, tiled=True)
+    rows, columns = partial_response.shape
+    blocks = partial_response.reshape(wide_count, rows // wide_count, narrow_count, columns // narrow_count)
+    blocks = blocks.transpose(0, 2, 1, 3).reshape(
+        wide_count * narrow_count, rows // wide_count, columns // narrow_count
+    )
+    gathered = lax.all_to_all(blocks, ("wide", "narrow"), 0, 0, tiled=True)
     return gathered.sum(0)
 
 

time: 287 us -> 322 us (1.12)
  the two profiles are of different devices: /device:TPU:57 before, /device:TPU:1 now
where the time goes in v1:
time: 322 us; the launch traced here: 316 us
  blocking collectives  114 us (35%)
  matrix products  84.7 us (26%)
  waiting for transfers between devices  54.6 us (17%)
  other arithmetic  28.3 us (9%)
  local copies, waits for them, and re-layouts  18.7 us (6%)
  starting transfers between devices  15.1 us (5%)
    all_to_all x1, blocking collectives, body(): gathered = lax.all_to_all(blocks, ('wide', 'narrow'), 0, 0, tiled=True)  114 us
    all_to_all x1, waiting for transfers between devices, body(): lax.all_to_all(sectioned_rows, 'narrow', split_axis=0, concat_axis=3, til...  44.2 us
    dot_general x9, matrix products, contract(): jnp.dot(rows[left_band][right_band], left_kron(occupied_blocks[left_band]...  38.8 us
    dot_general x36, matrix products, contract(): jnp.dot(source[:, piece * CHUNK:(piece + 1) * CHUNK], pieces[piece], pref...  32 us
    dot_general x1, matrix products, body(): lax.dot_general(left_product, right_product, (((1,), (1,)), ((), ())), pr...  13.9 us
    unnamed x3, other arithmetic  10.8 us
    ppermute x1, waiting for transfers between devices, neighbours(): before = lax.ppermute(array, axis, up)  10.4 us
    convert_element_type x1, other arithmetic, left_kron(): return (jnp.where(keep, full, 0.0) * row_mask[:, None]).astype(jnp.bfloat16)  9.05 us
  transfers between devices with their start and end apart: 3, of which 2 were waited for; matrix products, arithmetic and copies ran while one was open for 30% of the time, Pallas kernels for 0%

profile of v1, /device:TPU:1, one launch (start us, length us, event | category | flops | bytes accessed | tf_op | source)
XLA Modules:
  0.0 316.1 jit_solution(17365370531779497691)
XLA Ops:
  0.0 8.0 %all-to-all-start = ((bf16[8,1,3,128,1024]{4,3,2,1,0:T(8,128)(2,1)}), bf16[8,1,3,128,1024]{4,3,2,1,0:T(8,128)(2,1)}, u32[]{:S(2)}, u32[]{:S(2)}) async-start(bf16[8,1,3,128,1024]{4,3,2,1,0:T(8,128)(2,1)} %bitcast.392), calls=%async_computation | async-start | bytes 12582912 | tf_op jit(solution)/shard_map/all_to_all | solution.py:117
  26.0 9.1 %fusion.8 = (bf16[32,32,1024]{2,1,0:T(8,128)(2,1)}, bf16[32,32,1024]{2,1,0:T(8,128)(2,1)}, bf16[32,32,1024]{2,1,0:T(8,128)(2,1)}, bf16[32,32,1024]{2,1,0:T(8,128...) fusion(f32[32,32]{1,0:T(8,128)S(1)} %mul.367, ...), kind=kLoop, calls=%fused_computation.17 | loop fusion | flops 25165824 | bytes 19322880 | tf_op jit(solution)/shard_map/convert_element_type | solution.py:40
  35.1 44.2 %all-to-all-done = bf16[8,1,3,128,1024]{4,3,2,1,0:T(8,128)(2,1)} async-done(((bf16[8,1,3,128,1024]{4,3,2,1,0:T(8,128)(2,1)}), bf16[8,1,3,128,1024]{4,3,2,1,0:T(8,128)(2,1)}, u32[]{:S(2)}, u32[]{:S(2)}) %all-to-all-start) | async-done | bytes 6291488 | tf_op jit(solution)/shard_map/all_to_all | solution.py:117
  79.3 3.5 %copy.30 = bf16[8,1,3,128,1024]{4,3,0,2,1:T(8,128)(2,1)S(1)} copy(bf16[8,1,3,128,1024]{4,3,2,1,0:T(8,128)(2,1)} %all-to-all-done) | data formatting | bytes 12582912 | tf_op jit(solution)/shard_map/all_to_all | solution.py:117
  82.8 3.1 collective-permute-start
  85.8 4.1 %collective-permute-start.1 = (bf16[3,1024,1024]{2,1,0:T(8,128)(2,1)S(1)}, bf16[3,1024,1024]{2,1,0:T(8,128)(2,1)}, u32[]{:S(2)}, u32[]{:S(2)}) collective-permute-start(bf16[3,1024,1024]{2,1,0:T(8,128)(2,1)S(1)} %bitcast.362), channel_id=1, source_target_pairs={{1,0},{2,1},{3,2},{4,3},{5,4},{6,5},{7,6},{8,7},{9,8},{10,9},{11,1... | collective-permute-start | bytes 18874376 | tf_op jit(solution)/shard_map/ppermute | solution.py:109
  97.7 1.4 convolution_bitcast_fusion.17
  115.9 1.4 convolution_bitcast_fusion.8
  118.5 1.8 fusion.21
  120.2 3.9 %fusion.20 = bf16[1024,5120]{0,1:T(8,128)(2,1)} fusion(bf16[1024,5120]{0,1:T(8,128)(2,1)} %fusion.21, f32[1024,256]{0,1:T(8,128)S(1)} %convolution_bitcast_fusion.9, f32[1024,256]{0,1:T(8,128)S(1)} %convolution_bitcast_fusion.10, f32[1024,256]{0,1:T(8,128)S(1)} %convolution_bitcast_fusion.11, f32[1024,256]{0,1:T(8,128)S(1)} %convolution_bitcast_fusion.12, ...), kind=kLoop, calls=%fused_computation.37 | loop fusion | flops 12582912 | bytes 14680064
  124.1 5.2 %fusion.19 = bf16[1024,5120]{0,1:T(8,128)(2,1)} fusion(bf16[1024,5120]{0,1:T(8,128)(2,1)} %fusion.20, f32[1024,256]{0,1:T(8,128)} %convolution_bitcast_fusion.1, f32[1024,256]{0,1:T(8,128)} %convolution_bitcast_fusion.2, f32[1024,256]{0,1:T(8,128)} %convolution_bitcast_fusion.3, f32[1024,256]{0,1:T(8,128)} %convolution_bitcast_fusion.4, ...), kind=kLoop, calls=%fused_computation.36 | loop fusion | flops 8388608 | bytes 10485760
  134.1 4.4 %fusion.95 = f32[1024,1024]{1,0:T(8,128)} fusion(bf16[1024,1024]{1,0:T(8,128)(2,1)S(1)} %bitcast.401, bf16[1024,1024]{1,0:T(8,128)(2,1)S(1)} %bitcast.389), kind=kOutput, calls=%fused_computation.263 | convolution fusion | flops 2147483648 | bytes 8388608 | tf_op jit(solution)/shard_map/dot_general | solution.py:77
  138.5 2.4 fusion.96
  140.9 2.4 fusion.97
  143.3 10.4 %collective-permute-done = bf16[3,1024,1024]{2,1,0:T(8,128)(2,1)} collective-permute-done((bf16[3,1024,1024]{2,1,0:T(8,128)(2,1)S(1)}, bf16[3,1024,1024]{2,1,0:T(8,128)(2,1)}, u32[]{:S(2)}, u32[]{:S(2)}) %collective-permute-start) | collective-permute-done | bytes 6291488 | tf_op jit(solution)/shard_map/ppermute | solution.py:108
  153.7 4.1 %bitcast_dynamic-update-slice_fusion.1 = bf16[1024,5120]{0,1:T(8,128)(2,1)S(1)} fusion(bf16[1024,1024]{1,0:T(8,128)(2,1)S(1)} %bitcast.398, bf16[3,1024,1024]{2,1,0:T(8,128)(2,1)} %collective-permute-done), kind=kOutput, calls=%fused_computation.52 | convolution fusion | flops 2148532224 | bytes 6291456 | tf_op jit(solution)/shard_map/dot_general | solution.py:77
  157.9 6.4 %fusion.25 = f32[1024,1024]{1,0:T(8,128)} fusion(bf16[1024,1024]{1,0:T(8,128)(2,1)S(1)} %bitcast.397, bf16[3,1024,1024]{2,1,0:T(8,128)(2,1)} %collective-permute-done), kind=kOutput, calls=%fused_computation.46 | convolution fusion | flops 2147483648 | bytes 8388608 | tf_op jit(solution)/shard_map/dot_general | solution.py:77
  164.3 5.4 %fusion.14 = bf16[1024,5120]{0,1:T(8,128)(2,1)S(1)} fusion(bf16[1024,5120]{0,1:T(8,128)(2,1)S(1)} %bitcast_dynamic-update-slice_fusion.1, f32[1024,1024]{1,0:T(8,128)} %fusion.95, bf16[1024,1024]{1,0:T(8,128)(2,1)S(1)} %bitcast.396, bf16[3,1024,1024]{2,1,0:T(8,128)(2,1)} %collective-permute-done), kind=kOutput, calls=%fused_computation.31 | convolution fusion | flops 2149580800 | bytes 10485760 | tf_op jit(solution)/shard_map/dot_general | solution.py:77
  169.7 5.5 %fusion.16 = bf16[1024,5120]{0,1:T(8,128)(2,1)S(1)} fusion(bf16[1024,5120]{0,1:T(8,128)(2,1)S(1)} %fusion.14, f32[1024,1024]{1,0:T(8,128)} %fusion.25, f32[1024,1024]{1,0:T(8,128)S(1)} %fusion.96, bf16[1024,1024]{1,0:T(8,128)(2,1)S(1)} %bitcast.395, bf16[3,1024,1024]{2,1,0:T(8,128)(2,1)} %collective-permute-done.1), kind=kOutput, calls=%fused_computation.33 | convolution fusion | flops 2150629376 | bytes 14680064 | tf_op jit(solution)/shard_map/dot_general | solution.py:77
  175.2 4.2 %fusion.18 = bf16[1024,5120]{0,1:T(8,128)(2,1)S(1)} fusion(bf16[1024,5120]{0,1:T(8,128)(2,1)S(1)} %fusion.16, f32[1024,1024]{1,0:T(8,128)S(1)} %fusion.97, bf16[1024,1024]{1,0:T(8,128)(2,1)S(1)} %bitcast.394, bf16[3,1024,1024]{2,1,0:T(8,128)(2,1)} %collective-permute-done.1), kind=kOutput, calls=%fused_computation.35 | convolution fusion | flops 2149580800 | bytes 10485760 | tf_op jit(solution)/shard_map/dot_general | solution.py:77
  179.4 4.0 %bitcast_dynamic-update-slice_fusion = bf16[1024,5120]{0,1:T(8,128)(2,1)S(1)} fusion(bf16[1024,5120]{0,1:T(8,128)(2,1)S(1)} %fusion.18, bf16[1024,1024]{1,0:T(8,128)(2,1)S(1)} %bitcast.393, bf16[3,1024,1024]{2,1,0:T(8,128)(2,1)} %collective-permute-done.1), kind=kOutput, calls=%fused_computation.51 | convolution fusion | flops 2148532224 | bytes 6291456 | tf_op jit(solution)/shard_map/dot_general | solution.py:77
  183.4 13.9 %convolution_bitcast_fusion = f32[128,8,8,128]{3,1,2,0:T(8,128)S(1)} fusion(bf16[1024,5120]{0,1:T(8,128)(2,1)S(1)} %bitcast_dynamic-update-slice_fusion, bf16[1024,5120]{0,1:T(8,128)(2,1)} %fusion.43), kind=kOutput, calls=%fused_computation.29 | convolution fusion | flops 10737418240 | bytes 25165824 | tf_op jit(solution)/shard_map/dot_general | solution.py:138
  199.1 113.7 %all_to_all.20 = f32[256,32,128]{2,1,0:T(8,128)} all-to-all(f32[256,32,128]{2,1,0:T(8,128)S(1)} %bitcast.391), channel_id=1, replica_groups=mesh['wide'=32,'narrow'=8] {'wide','narrow'}, dimensions={0} | all-to-all | bytes 8388608 | tf_op jit(solution)/shard_map/all_to_all | solution.py:147
  312.8 3.1 reduce_sum.9
  (179 shorter events, 49.7 us)
Async XLA Ops:
  0.0 8.0 %copy-start.29 = (s32[256,3]{0,1:T(4,128)S(1)}, s32[256,3]{0,1:T(4,128)}, u32[]{:S(2)}) copy-start(s32[256,3]{0,1:T(4,128)} %param.11) | copy-start | bytes 9220
  0.0 8.2 %copy-start.28 = (s32[256,3]{0,1:T(4,128)S(1)}, s32[256,3]{0,1:T(4,128)}, u32[]{:S(2)}) copy-start(s32[256,3]{0,1:T(4,128)} %param.12) | copy-start | bytes 9220
  0.0 8.4 %copy-start.34 = (s32[256]{0:T(256)S(1)}, s32[256]{0:T(256)}, u32[]{:S(2)}) copy-start(s32[256]{0:T(256)} %param.10) | copy-start | bytes 3076
  0.0 10.9 %copy-start.13 = (bf16[256,3,1024]{2,0,1:T(8,128)(2,1)S(1)}, bf16[256,3,1024]{2,0,1:T(8,128)(2,1)}, u32[]{:S(2)}) copy-start(bf16[256,3,1024]{2,0,1:T(8,128)(2,1)} %param.8) | copy-start | bytes 4718596
  0.0 79.2 %all-to-all-start = ((bf16[8,1,3,128,1024]{4,3,2,1,0:T(8,128)(2,1)}), bf16[8,1,3,128,1024]{4,3,2,1,0:T(8,128)(2,1)}, u32[]{:S(2)}, u32[]{:S(2)}) async-start(bf16[8,1,3,128,1024]{4,3,2,1,0:T(8,128)(2,1)} %bitcast.392), calls=%async_computation | async-start | bytes 12582912 | tf_op jit(solution)/shard_map/all_to_all | solution.py:117
  8.0 12.6 %copy-start.14 = (bf16[256,3,1024]{2,0,1:T(8,128)(2,1)S(1)}, bf16[256,3,1024]{2,0,1:T(8,128)(2,1)}, u32[]{:S(2)}) copy-start(bf16[256,3,1024]{2,0,1:T(8,128)(2,1)} %param.9) | copy-start | bytes 4718596
  11.0 9.4 %copy-start.30 = (s32[3]{0:T(128)S(1)}, s32[3]{0:T(128)}, u32[]{:S(2)}) copy-start(s32[3]{0:T(128)} %get-tuple-element.78) | copy-start | bytes 40
  11.0 9.4 %copy-start.31 = (s32[1,3]{1,0:T(1,128)S(1)}, s32[1,3]{1,0:T(1,128)}, u32[]{:S(2)}) copy-start(s32[1,3]{1,0:T(1,128)} %get-tuple-element.80) | copy-start | bytes 40
  11.0 9.4 %copy-start.32 = (s32[1,3]{1,0:T(1,128)S(1)}, s32[1,3]{1,0:T(1,128)}, u32[]{:S(2)}) copy-start(s32[1,3]{1,0:T(1,128)} %get-tuple-element.81) | copy-start | bytes 40
  11.0 9.4 %copy-start.33 = (s32[1,3]{1,0:T(1,128)S(1)}, s32[1,3]{1,0:T(1,128)}, u32[]{:S(2)}) copy-start(s32[1,3]{1,0:T(1,128)} %get-tuple-element.82) | copy-start | bytes 40
  11.4 10.3 %copy-start.27 = (f32[1,1,1024]{2,1,0:T(1,128)S(1)}, f32[1,1,1024]{2,1,0:T(1,128)}, u32[]{:S(2)}) copy-start(f32[1,1,1024]{2,1,0:T(1,128)} %get-tuple-element.40) | copy-start | bytes 12292
  11.5 10.4 %copy-start.26 = (f32[1,1,1024]{2,1,0:T(1,128)S(1)}, f32[1,1,1024]{2,1,0:T(1,128)}, u32[]{:S(2)}) copy-start(f32[1,1,1024]{2,1,0:T(1,128)} %get-tuple-element.50) | copy-start | bytes 12292
  11.5 10.4 %copy-start.25 = (f32[1,1,1024]{2,1,0:T(1,128)S(1)}, f32[1,1,1024]{2,1,0:T(1,128)}, u32[]{:S(2)}) copy-start(f32[1,1,1024]{2,1,0:T(1,128)} %get-tuple-element.39) | copy-start | bytes 12292
  24.7 71.4 %copy-start.12 = (bf16[4,256,256]{2,1,0:T(8,128)(2,1)}, bf16[4,256,256]{2,1,0:T(8,128)(2,1)S(1)}, u32[]{:S(2)}) copy-start(bf16[4,256,256]{2,1,0:T(8,128)(2,1)S(1)} %get-tuple-element.64) | copy-start | bytes 1572868
  82.8 71.0 %collective-permute-start = (bf16[3,1024,1024]{2,1,0:T(8,128)(2,1)S(1)}, bf16[3,1024,1024]{2,1,0:T(8,128)(2,1)}, u32[]{:S(2)}, u32[]{:S(2)}) collective-permute-start(bf16[3,1024,1024]{2,1,0:T(8,128)(2,1)S(1)} %bitcast.361), channel_id=1, source_target_pairs={{0,1},{1,2},{2,3},{3,4},{4,5},{5,6},{6,7},{7,8},{8,9},{9,10},{10,1... | collective-permute-start | bytes 18874376 | tf_op jit(solution)/shard_map/ppermute | solution.py:108
  85.8 83.8 %collective-permute-start.1 = (bf16[3,1024,1024]{2,1,0:T(8,128)(2,1)S(1)}, bf16[3,1024,1024]{2,1,0:T(8,128)(2,1)}, u32[]{:S(2)}, u32[]{:S(2)}) collective-permute-start(bf16[3,1024,1024]{2,1,0:T(8,128)(2,1)S(1)} %bitcast.362), channel_id=1, source_target_pairs={{1,0},{2,1},{3,2},{4,3},{5,4},{6,5},{7,6},{8,7},{9,8},{10,9},{11,1... | collective-permute-start | bytes 18874376 | tf_op jit(solution)/shard_map/ppermute | solution.py:109
  96.4 6.7 %copy-start.16 = (bf16[4,256,256]{2,1,0:T(8,128)(2,1)S(1)}, bf16[4,256,256]{2,1,0:T(8,128)(2,1)}, u32[]{:S(2)}) copy-start(bf16[4,256,256]{2,1,0:T(8,128)(2,1)} %get-tuple-element.68) | copy-start | bytes 1572868
  99.1 7.4 %copy-start.11 = (bf16[4,256,256]{2,1,0:T(8,128)(2,1)S(1)}, bf16[4,256,256]{2,1,0:T(8,128)(2,1)}, u32[]{:S(2)}) copy-start(bf16[4,256,256]{2,1,0:T(8,128)(2,1)} %get-tuple-element.61) | copy-start | bytes 1572868
  105.4 6.6 %copy-start.9 = (bf16[4,256,256]{2,1,0:T(8,128)(2,1)S(1)}, bf16[4,256,256]{2,1,0:T(8,128)(2,1)}, u32[]{:S(2)}) copy-start(bf16[4,256,256]{2,1,0:T(8,128)(2,1)} %get-tuple-element.63) | copy-start | bytes 1572868
  124.1 5.3 %copy-start.15 = (bf16[4,256,256]{2,1,0:T(8,128)(2,1)S(1)}, bf16[4,256,256]{2,1,0:T(8,128)(2,1)}, u32[]{:S(2)}) copy-start(bf16[4,256,256]{2,1,0:T(8,128)(2,1)} %get-tuple-element.60) | copy-start | bytes 1572868
  140.9 12.8 %copy-start.5 = (bf16[32,32,1024]{2,1,0:T(8,128)(2,1)S(1)}, bf16[32,32,1024]{2,1,0:T(8,128)(2,1)}, u32[]{:S(2)}) copy-start(bf16[32,32,1024]{2,1,0:T(8,128)(2,1)} %get-tuple-element.57) | copy-start | bytes 6291460
  157.9 6.4 %copy-start.3 = (bf16[32,32,1024]{2,1,0:T(8,128)(2,1)S(1)}, bf16[32,32,1024]{2,1,0:T(8,128)(2,1)}, u32[]{:S(2)}) copy-start(bf16[32,32,1024]{2,1,0:T(8,128)(2,1)} %get-tuple-element.58) | copy-start | bytes 6291460
  164.3 5.4 %copy-start.2 = (bf16[32,32,1024]{2,1,0:T(8,128)(2,1)S(1)}, bf16[32,32,1024]{2,1,0:T(8,128)(2,1)}, u32[]{:S(2)}) copy-start(bf16[32,32,1024]{2,1,0:T(8,128)(2,1)} %get-tuple-element.23) | copy-start | bytes 6291460
  169.7 5.5 %copy-start.1 = (bf16[32,32,1024]{2,1,0:T(8,128)(2,1)S(1)}, bf16[32,32,1024]{2,1,0:T(8,128)(2,1)}, u32[]{:S(2)}) copy-start(bf16[32,32,1024]{2,1,0:T(8,128)(2,1)} %get-tuple-element.22) | copy-start | bytes 6291460
  (14 other events, 53.0 us)

commit v2 on v0

--- a/solution.py
+++ b/solution.py
@@ -138,7 +138,11 @@
     partial_response = lax.dot_general(
         left_product, right_product, (((1,), (1,)), ((), ())), preferred_element_type=jnp.float32
     )
-    column_share = lax.psum_scatter(partial_response, "narrow", scatter_dimension=1, tiled=True)
+    rows, columns = partial_response.shape
+    column_blocks = partial_response.reshape(rows, narrow_count, columns // narrow_count).transpose(1, 0, 2)
+    column_share = lax.psum_scatter(
+        column_blocks.reshape(narrow_count * rows, columns // narrow_count), "narrow", scatter_dimension=0, tiled=True
+    )
     wide_count = lax.axis_size("wide")
     row_pieces = column_share.reshape(wide_count, column_share.shape[0] // wide_count, column_share.shape[1])
     gathered = lax.all_to_all(row_pieces, "wide", 0, 0, tiled=True)

time: 287 us -> 292 us (1.017)
  local copies, waits for them, and re-layouts: 15.7 us -> 21 us
    reshape x0 -> x1, local copies, waits for them, and re-layouts: none -> 5.33 us  [body(): partial_response.reshape(rows, narrow_count, columns // narrow_count)]
  transfers between devices with their start and end apart: 4 -> 4, of which waited for: 3 -> 3; matrix products, arithmetic and copies ran while one was open for 34% -> 33% of each run, Pallas kernels for 0% -> 0%
where the time goes in v2:
time: 292 us; the launch traced here: 287 us
  waiting for transfers between devices  98.6 us (34%)
  matrix products  88.3 us (30%)
  blocking collectives  27.1 us (9%)
  other arithmetic  24.4 us (8%)
  local copies, waits for them, and re-layouts  21 us (7%)
  between operations  14.3 us (5%)
  starting transfers between devices  13.4 us (5%)
    all_to_all x1, waiting for transfers between devices, body(): lax.all_to_all(sectioned_rows, 'narrow', split_axis=0, concat_axis=3, til...  45.2 us
    reduce_scatter x1, waiting for transfers between devices, body(): lax.psum_scatter(column_blocks.reshape(narrow_count * rows, columns // na...  42.8 us
    dot_general x9, matrix products, contract(): jnp.dot(rows[left_band][right_band], left_kron(occupied_blocks[left_band]...  39 us
    dot_general x36, matrix products, contract(): jnp.dot(source[:, piece * CHUNK:(piece + 1) * CHUNK], pieces[piece], pref...  33.9 us
    all_to_all x1, blocking collectives, body(): gathered = lax.all_to_all(row_pieces, 'wide', 0, 0, tiled=True)  27.1 us
    dot_general x1, matrix products, body(): lax.dot_general(left_product, right_product, (((1,), (1,)), ((), ())), pr...  15.4 us
    unnamed x3, other arithmetic  10.9 us
    ppermute x1, waiting for transfers between devices, neighbours(): before = lax.ppermute(array, axis, up)  10.5 us
  transfers between devices with their start and end apart: 4, of which 3 were waited for; matrix products, arithmetic and copies ran while one was open for 33% of the time, Pallas kernels for 0%

profile of v2, /device:TPU:57, one launch (start us, length us, event | category | flops | bytes accessed | tf_op | source)
XLA Modules:
  0.0 287.0 jit_solution(9262915605001201986)
XLA Ops:
  6.5 5.3 %all-to-all-start = ((bf16[8,1,3,128,1024]{4,3,2,1,0:T(8,128)(2,1)}), bf16[8,1,3,128,1024]{4,3,2,1,0:T(8,128)(2,1)}, u32[]{:S(2)}, u32[]{:S(2)}) async-start(bf16[8,1,3,128,1024]{4,3,2,1,0:T(8,128)(2,1)} %bitcast.389), calls=%async_computation | async-start | bytes 12582912 | tf_op jit(solution)/shard_map/all_to_all | solution.py:117
  27.1 9.1 %fusion.8 = (bf16[32,32,1024]{2,1,0:T(8,128)(2,1)}, bf16[32,32,1024]{2,1,0:T(8,128)(2,1)}, bf16[32,32,1024]{2,1,0:T(8,128)(2,1)}, bf16[32,32,1024]{2,1,0:T(8,128...) fusion(f32[32,32]{1,0:T(8,128)S(1)} %mul.367, ...), kind=kLoop, calls=%fused_computation.17 | loop fusion | flops 25165824 | bytes 19322880 | tf_op jit(solution)/shard_map/convert_element_type | solution.py:40
  36.2 45.2 %all-to-all-done = bf16[8,1,3,128,1024]{4,3,2,1,0:T(8,128)(2,1)} async-done(((bf16[8,1,3,128,1024]{4,3,2,1,0:T(8,128)(2,1)}), bf16[8,1,3,128,1024]{4,3,2,1,0:T(8,128)(2,1)}, u32[]{:S(2)}, u32[]{:S(2)}) %all-to-all-start) | async-done | bytes 6291488 | tf_op jit(solution)/shard_map/all_to_all | solution.py:117
  81.4 3.5 %copy.29 = bf16[8,1,3,128,1024]{4,3,0,2,1:T(8,128)(2,1)S(1)} copy(bf16[8,1,3,128,1024]{4,3,2,1,0:T(8,128)(2,1)} %all-to-all-done) | data formatting | bytes 12582912 | tf_op jit(solution)/shard_map/all_to_all | solution.py:117
  84.9 5.9 %collective-permute-start = (bf16[3,1024,1024]{2,1,0:T(8,128)(2,1)S(1)}, bf16[3,1024,1024]{2,1,0:T(8,128)(2,1)}, u32[]{:S(2)}, u32[]{:S(2)}) collective-permute-start(bf16[3,1024,1024]{2,1,0:T(8,128)(2,1)S(1)} %bitcast.359), channel_id=1, source_target_pairs={{0,1},{1,2},{2,3},{3,4},{4,5},{5,6},{6,7},{7,8},{8,9},{9,10},{10,1... | collective-permute-start | bytes 18874376 | tf_op jit(solution)/shard_map/ppermute | solution.py:108
  90.8 2.1 collective-permute-start.1
  100.2 2.4 convolution_bitcast_fusion.15
  123.3 1.8 fusion.21
  125.1 4.2 %fusion.20 = bf16[1024,5120]{0,1:T(8,128)(2,1)} fusion(bf16[1024,5120]{0,1:T(8,128)(2,1)} %fusion.21, f32[1024,256]{0,1:T(8,128)S(1)} %convolution_bitcast_fusion.8, f32[1024,256]{0,1:T(8,128)S(1)} %convolution_bitcast_fusion.9, f32[1024,256]{0,1:T(8,128)S(1)} %convolution_bitcast_fusion.10, f32[1024,256]{0,1:T(8,128)S(1)} %convolution_bitcast_fusion.11, ...), kind=kLoop, calls=%fused_computation.36 | loop fusion | flops 12582912 | bytes 14680064
  129.2 5.0 %fusion.19 = bf16[1024,5120]{0,1:T(8,128)(2,1)} fusion(bf16[1024,5120]{0,1:T(8,128)(2,1)} %fusion.20, f32[1024,256]{0,1:T(8,128)} %convolution_bitcast_fusion, f32[1024,256]{0,1:T(8,128)} %convolution_bitcast_fusion.1, f32[1024,256]{0,1:T(8,128)} %convolution_bitcast_fusion.2, f32[1024,256]{0,1:T(8,128)} %convolution_bitcast_fusion.3, ...), kind=kLoop, calls=%fused_computation.35 | loop fusion | flops 8388608 | bytes 10485760
  139.0 4.4 %fusion.95 = f32[1024,1024]{1,0:T(8,128)} fusion(bf16[1024,1024]{1,0:T(8,128)(2,1)S(1)} %bitcast.399, bf16[1024,1024]{1,0:T(8,128)(2,1)S(1)} %bitcast.387), kind=kOutput, calls=%fused_computation.262 | convolution fusion | flops 2147483648 | bytes 8388608 | tf_op jit(solution)/shard_map/dot_general | solution.py:77
  143.4 2.4 fusion.96
  145.8 2.4 fusion.97
  148.2 10.5 %collective-permute-done = bf16[3,1024,1024]{2,1,0:T(8,128)(2,1)} collective-permute-done((bf16[3,1024,1024]{2,1,0:T(8,128)(2,1)S(1)}, bf16[3,1024,1024]{2,1,0:T(8,128)(2,1)}, u32[]{:S(2)}, u32[]{:S(2)}) %collective-permute-start) | collective-permute-done | bytes 6291488 | tf_op jit(solution)/shard_map/ppermute | solution.py:108
  158.7 4.1 %bitcast_dynamic-update-slice_fusion.1 = bf16[1024,5120]{0,1:T(8,128)(2,1)S(1)} fusion(bf16[1024,1024]{1,0:T(8,128)(2,1)S(1)} %bitcast.396, bf16[3,1024,1024]{2,1,0:T(8,128)(2,1)} %collective-permute-done), kind=kOutput, calls=%fused_computation.51 | convolution fusion | flops 2148532224 | bytes 6291456 | tf_op jit(solution)/shard_map/dot_general | solution.py:77
  162.9 6.6 %fusion.25 = f32[1024,1024]{1,0:T(8,128)} fusion(bf16[1024,1024]{1,0:T(8,128)(2,1)S(1)} %bitcast.395, bf16[3,1024,1024]{2,1,0:T(8,128)(2,1)} %collective-permute-done), kind=kOutput, calls=%fused_computation.45 | convolution fusion | flops 2147483648 | bytes 8388608 | tf_op jit(solution)/shard_map/dot_general | solution.py:77
  169.5 5.4 %fusion.14 = bf16[1024,5120]{0,1:T(8,128)(2,1)S(1)} fusion(bf16[1024,5120]{0,1:T(8,128)(2,1)S(1)} %bitcast_dynamic-update-slice_fusion.1, f32[1024,1024]{1,0:T(8,128)} %fusion.95, bf16[1024,1024]{1,0:T(8,128)(2,1)S(1)} %bitcast.394, bf16[3,1024,1024]{2,1,0:T(8,128)(2,1)} %collective-permute-done), kind=kOutput, calls=%fused_computation.30 | convolution fusion | flops 2149580800 | bytes 10485760 | tf_op jit(solution)/shard_map/dot_general | solution.py:77
  174.9 5.5 %fusion.16 = bf16[1024,5120]{0,1:T(8,128)(2,1)S(1)} fusion(bf16[1024,5120]{0,1:T(8,128)(2,1)S(1)} %fusion.14, f32[1024,1024]{1,0:T(8,128)} %fusion.25, f32[1024,1024]{1,0:T(8,128)S(1)} %fusion.96, bf16[1024,1024]{1,0:T(8,128)(2,1)S(1)} %bitcast.393, bf16[3,1024,1024]{2,1,0:T(8,128)(2,1)} %collective-permute-done.1), kind=kOutput, calls=%fused_computation.32 | convolution fusion | flops 2150629376 | bytes 14680064 | tf_op jit(solution)/shard_map/dot_general | solution.py:77
  180.4 4.2 %fusion.18 = bf16[1024,5120]{0,1:T(8,128)(2,1)S(1)} fusion(bf16[1024,5120]{0,1:T(8,128)(2,1)S(1)} %fusion.16, f32[1024,1024]{1,0:T(8,128)S(1)} %fusion.97, bf16[1024,1024]{1,0:T(8,128)(2,1)S(1)} %bitcast.392, bf16[3,1024,1024]{2,1,0:T(8,128)(2,1)} %collective-permute-done.1), kind=kOutput, calls=%fused_computation.34 | convolution fusion | flops 2149580800 | bytes 10485760 | tf_op jit(solution)/shard_map/dot_general | solution.py:77
  184.6 4.0 %bitcast_dynamic-update-slice_fusion = bf16[1024,5120]{0,1:T(8,128)(2,1)S(1)} fusion(bf16[1024,5120]{0,1:T(8,128)(2,1)S(1)} %fusion.18, bf16[1024,1024]{1,0:T(8,128)(2,1)S(1)} %bitcast.391, bf16[3,1024,1024]{2,1,0:T(8,128)(2,1)} %collective-permute-done.1), kind=kOutput, calls=%fused_computation.50 | convolution fusion | flops 2148532224 | bytes 6291456 | tf_op jit(solution)/shard_map/dot_general | solution.py:77
  188.6 15.4 %fusion.98 = f32[1024,1024]{0,1:T(8,128)} fusion(bf16[1024,5120]{0,1:T(8,128)(2,1)S(1)} %bitcast_dynamic-update-slice_fusion, bf16[1024,5120]{0,1:T(8,128)(2,1)} %fusion.43), kind=kOutput, calls=%fused_computation.265 | convolution fusion | flops 10737418240 | bytes 25165824 | tf_op jit(solution)/shard_map/dot_general | solution.py:138
  204.0 5.3 %copy.26 = f32[1024,8,128]{2,0,1:T(8,128)} copy(f32[1024,8,128]{0,2,1:T(8,128)} %bitcast.390) | data formatting | bytes 8388608 | tf_op jit(solution)/shard_map/reshape | solution.py:142
  209.4 42.8 %reduce-scatter.2.cloned.1.call-done = f32[1024,128]{1,0:T(8,128)} async-done(((f32[8192,128]{1,0:T(8,128)}), f32[1024,128]{1,0:T(8,128)}) %reduce-scatter.2.cloned.1.call-update) | async-done | bytes 524304 | tf_op jit(solution)/shard_map/reduce_scatter | solution.py:143
  252.2 27.1 %all_to_all.20 = f32[32,32,128]{2,1,0:T(8,128)S(1)} all-to-all(f32[32,32,128]{2,1,0:T(8,128)} %bitcast.400), channel_id=1, replica_groups=mesh['wide'=32,'narrow'=8] {'wide'}, dimensions={0} | all-to-all | bytes 1048576 | tf_op jit(solution)/shard_map/all_to_all | solution.py:148
  (173 shorter events, 48.1 us)
Async XLA Ops:
  6.5 5.4 %copy-start.29 = (s32[256,3]{0,1:T(4,128)S(1)}, s32[256,3]{0,1:T(4,128)}, u32[]{:S(2)}) copy-start(s32[256,3]{0,1:T(4,128)} %param.11) | copy-start | bytes 9220
  6.5 5.6 %copy-start.28 = (s32[256,3]{0,1:T(4,128)S(1)}, s32[256,3]{0,1:T(4,128)}, u32[]{:S(2)}) copy-start(s32[256,3]{0,1:T(4,128)} %param.12) | copy-start | bytes 9220
  6.5 5.8 %copy-start.30 = (s32[256]{0:T(256)S(1)}, s32[256]{0:T(256)}, u32[]{:S(2)}) copy-start(s32[256]{0:T(256)} %param.10) | copy-start | bytes 3076
  6.5 6.6 %copy-start.12 = (bf16[256,3,1024]{2,0,1:T(8,128)(2,1)S(1)}, bf16[256,3,1024]{2,0,1:T(8,128)(2,1)}, u32[]{:S(2)}) copy-start(bf16[256,3,1024]{2,0,1:T(8,128)(2,1)} %param.8) | copy-start | bytes 4718596
  6.5 74.9 %all-to-all-start = ((bf16[8,1,3,128,1024]{4,3,2,1,0:T(8,128)(2,1)}), bf16[8,1,3,128,1024]{4,3,2,1,0:T(8,128)(2,1)}, u32[]{:S(2)}, u32[]{:S(2)}) async-start(bf16[8,1,3,128,1024]{4,3,2,1,0:T(8,128)(2,1)} %bitcast.389), calls=%async_computation | async-start | bytes 12582912 | tf_op jit(solution)/shard_map/all_to_all | solution.py:117
  11.9 10.3 %copy-start.27 = (s32[256,3]{0,1:T(4,128)S(1)}, s32[256,3]{0,1:T(4,128)}, u32[]{:S(2)}) copy-start(s32[256,3]{0,1:T(4,128)} %param.13) | copy-start | bytes 9220
  11.9 10.7 %copy-start.13 = (bf16[256,3,1024]{2,0,1:T(8,128)(2,1)S(1)}, bf16[256,3,1024]{2,0,1:T(8,128)(2,1)}, u32[]{:S(2)}) copy-start(bf16[256,3,1024]{2,0,1:T(8,128)(2,1)} %param.9) | copy-start | bytes 4718596
  11.9 240.3 %reduce-scatter.2.cloned.1.call-start = ((), (), s32[]{:S(2)}) async-start(), calls=%async_computation.3 | async-start | bytes 4718592 | tf_op jit(solution)/shard_map/reduce_scatter | solution.py:143
  24.1 2.9 %copy-start.14 = (f32[32,1024]{1,0:T(8,128)S(1)}, f32[32,1024]{1,0:T(8,128)}, u32[]{:S(2)}) copy-start(f32[32,1024]{1,0:T(8,128)} %broadcast_in_dim.71) | copy-start | bytes 393220
  25.7 72.9 %copy-start.11 = (bf16[4,256,256]{2,1,0:T(8,128)(2,1)}, bf16[4,256,256]{2,1,0:T(8,128)(2,1)S(1)}, u32[]{:S(2)}) copy-start(bf16[4,256,256]{2,1,0:T(8,128)(2,1)S(1)} %get-tuple-element.64) | copy-start | bytes 1572868
  84.9 73.8 %collective-permute-start = (bf16[3,1024,1024]{2,1,0:T(8,128)(2,1)S(1)}, bf16[3,1024,1024]{2,1,0:T(8,128)(2,1)}, u32[]{:S(2)}, u32[]{:S(2)}) collective-permute-start(bf16[3,1024,1024]{2,1,0:T(8,128)(2,1)S(1)} %bitcast.359), channel_id=1, source_target_pairs={{0,1},{1,2},{2,3},{3,4},{4,5},{5,6},{6,7},{7,8},{8,9},{9,10},{10,1... | collective-permute-start | bytes 18874376 | tf_op jit(solution)/shard_map/ppermute | solution.py:108
  90.8 84.1 %collective-permute-start.1 = (bf16[3,1024,1024]{2,1,0:T(8,128)(2,1)S(1)}, bf16[3,1024,1024]{2,1,0:T(8,128)(2,1)}, u32[]{:S(2)}, u32[]{:S(2)}) collective-permute-start(bf16[3,1024,1024]{2,1,0:T(8,128)(2,1)S(1)} %bitcast.360), channel_id=1, source_target_pairs={{1,0},{2,1},{3,2},{4,3},{5,4},{6,5},{7,6},{8,7},{9,8},{10,9},{11,1... | collective-permute-start | bytes 18874376 | tf_op jit(solution)/shard_map/ppermute | solution.py:109
  97.9 4.7 %copy-start.9 = (bf16[4,256,256]{2,1,0:T(8,128)(2,1)S(1)}, bf16[4,256,256]{2,1,0:T(8,128)(2,1)}, u32[]{:S(2)}) copy-start(bf16[4,256,256]{2,1,0:T(8,128)(2,1)} %get-tuple-element.66) | copy-start | bytes 1572868
  100.2 7.7 %copy-start.18 = (bf16[4,256,256]{2,1,0:T(8,128)(2,1)S(1)}, bf16[4,256,256]{2,1,0:T(8,128)(2,1)}, u32[]{:S(2)}) copy-start(bf16[4,256,256]{2,1,0:T(8,128)(2,1)} %get-tuple-element.68) | copy-start | bytes 1572868
  103.9 7.4 %copy-start.10 = (bf16[4,256,256]{2,1,0:T(8,128)(2,1)S(1)}, bf16[4,256,256]{2,1,0:T(8,128)(2,1)}, u32[]{:S(2)}) copy-start(bf16[4,256,256]{2,1,0:T(8,128)(2,1)} %get-tuple-element.61) | copy-start | bytes 1572868
  129.2 5.0 %copy-start.17 = (bf16[4,256,256]{2,1,0:T(8,128)(2,1)S(1)}, bf16[4,256,256]{2,1,0:T(8,128)(2,1)}, u32[]{:S(2)}) copy-start(bf16[4,256,256]{2,1,0:T(8,128)(2,1)} %get-tuple-element.60) | copy-start | bytes 1572868
  134.3 4.7 %copy-start.8 = (bf16[32,32,1024]{2,1,0:T(8,128)(2,1)S(1)}, bf16[32,32,1024]{2,1,0:T(8,128)(2,1)}, u32[]{:S(2)}) copy-start(bf16[32,32,1024]{2,1,0:T(8,128)(2,1)} %get-tuple-element.54) | copy-start | bytes 6291460
  139.0 4.4 %copy-start.7 = (bf16[32,32,1024]{2,1,0:T(8,128)(2,1)S(1)}, bf16[32,32,1024]{2,1,0:T(8,128)(2,1)}, u32[]{:S(2)}) copy-start(bf16[32,32,1024]{2,1,0:T(8,128)(2,1)} %get-tuple-element.55) | copy-start | bytes 6291460
  145.8 12.9 %copy-start.5 = (bf16[32,32,1024]{2,1,0:T(8,128)(2,1)S(1)}, bf16[32,32,1024]{2,1,0:T(8,128)(2,1)}, u32[]{:S(2)}) copy-start(bf16[32,32,1024]{2,1,0:T(8,128)(2,1)} %get-tuple-element.57) | copy-start | bytes 6291460
  158.7 4.1 %copy-start.4 = (bf16[32,32,1024]{2,1,0:T(8,128)(2,1)S(1)}, bf16[32,32,1024]{2,1,0:T(8,128)(2,1)}, u32[]{:S(2)}) copy-start(bf16[32,32,1024]{2,1,0:T(8,128)(2,1)} %get-tuple-element.59) | copy-start | bytes 6291460
  162.9 6.6 %copy-start.3 = (bf16[32,32,1024]{2,1,0:T(8,128)(2,1)S(1)}, bf16[32,32,1024]{2,1,0:T(8,128)(2,1)}, u32[]{:S(2)}) copy-start(bf16[32,32,1024]{2,1,0:T(8,128)(2,1)} %get-tuple-element.58) | copy-start | bytes 6291460
  169.5 5.4 %copy-start.2 = (bf16[32,32,1024]{2,1,0:T(8,128)(2,1)S(1)}, bf16[32,32,1024]{2,1,0:T(8,128)(2,1)}, u32[]{:S(2)}) copy-start(bf16[32,32,1024]{2,1,0:T(8,128)(2,1)} %get-tuple-element.23) | copy-start | bytes 6291460
  174.9 5.5 %copy-start.1 = (bf16[32,32,1024]{2,1,0:T(8,128)(2,1)S(1)}, bf16[32,32,1024]{2,1,0:T(8,128)(2,1)}, u32[]{:S(2)}) copy-start(bf16[32,32,1024]{2,1,0:T(8,128)(2,1)} %get-tuple-element.22) | copy-start | bytes 6291460
  180.4 4.2 %copy-start = (bf16[32,32,1024]{2,1,0:T(8,128)(2,1)S(1)}, bf16[32,32,1024]{2,1,0:T(8,128)(2,1)}, u32[]{:S(2)}) copy-start(bf16[32,32,1024]{2,1,0:T(8,128)(2,1)} %get-tuple-element.21) | copy-start | bytes 6291460
  (11 other events, 31.4 us)
Sparse Core Ops, SparseCore 0:
  209.5 42.6 reduce-scatter.1
